TPU v7x, 128 devices: a whole 4x4x4 slice. The times are simulated.
128 devices in a mesh: dp: 8 (over x_hi, z), tensor: 16 (over y, x_lo, core).
Axes of the slice: x: 4 (x_hi: 2, x_lo: 2; x = x_hi * 2 + x_lo), y: 4, z: 4, core: 2. Of those that a mesh axis runs over, the one named last changes fastest.
Arguments:
- tokens: bfloat16 [16384, 2048], P(('dp', 'tensor')), parts along dimension 0, may hold values from -6 to 6
- segment_ids: int32 [16384], P('dp'), parts along dimension 0, may hold values from 0 to 3, never falling along the last dimension, each value on 1 to 1024 neighbouring positions
- attention_gain: float32 [2048], replicated, may hold values from 0.1 to 1.9
- query_weight: bfloat16 [2048, 2048], P(None, 'tensor'), may hold values from -1 to 1
- key_weight: bfloat16 [2048, 2048], P(None, 'tensor'), may hold values from -1 to 1
- value_weight: bfloat16 [2048, 2048], P(None, 'tensor'), may hold values from -0.125 to 0.125
- output_weight: bfloat16 [2048, 2048], P('tensor'), may hold values from -0.125 to 0.125
- ffn_gain: float32 [2048], replicated, may hold values from 0.1 to 1.9
- shared_gate: bfloat16 [2048, 2816], P(None, 'tensor'), may hold values from -0.125 to 0.125
- shared_up: bfloat16 [2048, 2816], P(None, 'tensor'), may hold values from -0.125 to 0.125
- shared_down: bfloat16 [2816, 2048], P('tensor'), may hold values from -0.109375 to 0.109375
- expert_gate: bfloat16 [16, 2048, 1408], P('tensor'), may hold values from -0.125 to 0.125
- expert_up: bfloat16 [16, 2048, 1408], P('tensor'), may hold values from -0.125 to 0.125
- expert_down: bfloat16 [16, 1408, 2048], P('tensor'), may hold values from -0.15625 to 0.15625
- expert_ids: int32 [16384, 6], P('dp'), parts along dimension 0, may hold values from 0 to 15, all different within a row; in each aligned block of 128 rows (0 to 127, 128 to 255, ...) at most 64 rows name the same one
- gate_weights: float32 [16384, 6], P('dp'), parts along dimension 0, may hold values from 0.05 to 0.35
- page_table: int32 [128], P('dp'), parts along dimension 0, may hold values from 0 to 15, each once
Outputs:
- layer_out: bfloat16 [16384, 2048], P(('dp', 'tensor')), parts along dimension 0
- kv_pages: bfloat16 [2, 128, 128, 2048], P(None, 'dp', None, 'tensor'), parts along dimension 1
There are 8 independent parts, one for each index of `dp`. A program takes and returns all parts, laid end to end along the dimension named above; an argument that names none is the same for every part. Nothing has to cross between parts.
Inputs may be any that keep to these rules, and one draw needn't show every extreme that they name: `segment_ids`: ids never fall along the stream; each of the 4 prompts holds 1 to 1024 tokens and one holds exactly 1024. `expert_ids`: each row names 6 different experts; within each aligned block of 128 rows (the tokens of one index of tensor) no expert is named by more than 64 rows, a bound that some block reaches. `page_table`: each cache page is named once.
All inputs are finite; a program needn't handle non-finite values.
Results may differ from a plain program's by a relative error of at most 0.02.
The roundings to bfloat16 on the way count: a program that leaves them out, or rounds other values in their place, can miss the bound.
Values may be sent and summed in bfloat16 or wider, within the bound.
No kernel may reach another device: no remote copies, remote signals or barrier semaphores. Data moves between devices by JAX's collectives and lax.ppermute only.
A program may use at most 128 MiB of HBM per device.

v0:
```python
import jax
import jax.numpy as jnp
from jax import lax
from jax.sharding import PartitionSpec as P

HD = 128
TOP = 6
PAGE = 128


def rms_scale(hidden, gain):
    widened = hidden.astype(jnp.float32)
    inverse = lax.rsqrt(jnp.mean(widened * widened, axis=-1, keepdims=True) + 1e-06)
    return (widened * inverse * gain).astype(jnp.bfloat16)


def attend(projected, segment_ids, head_count):
    total_tokens = projected.shape[0]
    inner = head_count * HD
    queries = projected[:, :inner].reshape(total_tokens, head_count, HD)
    keys = projected[:, inner : 2 * inner].reshape(total_tokens, head_count, HD)
    values = projected[:, 2 * inner :].reshape(total_tokens, head_count, HD)
    scale = HD ** (-0.5)
    positions = jnp.arange(total_tokens, dtype=jnp.int32)
    span = min(512, total_tokens)

    def one_block(start):
        query_rows = lax.dynamic_slice_in_dim(queries, start, span, 0)
        query_segments = lax.dynamic_slice_in_dim(segment_ids, start, span, 0)
        query_positions = start + jnp.arange(span, dtype=jnp.int32)
        scores = (
            jnp.einsum("qhd,khd->hqk", query_rows, keys, preferred_element_type=jnp.float32) * scale
        )
        allowed = (query_segments[:, None] == segment_ids[None, :]) & (
            positions[None, :] <= query_positions[:, None]
        )
        scores = jnp.where(allowed[None], scores, -jnp.inf)
        highest = jnp.max(scores, axis=-1, keepdims=True)
        weights = jnp.exp(scores - highest)
        probs = (weights / jnp.sum(weights, axis=-1, keepdims=True)).astype(jnp.bfloat16)
        context = jnp.einsum("hqk,khd->qhd", probs, values, preferred_element_type=jnp.float32)
        return context.astype(jnp.bfloat16)

    starts = jnp.arange(total_tokens // span, dtype=jnp.int32) * span
    context = lax.map(one_block, starts).reshape(total_tokens, inner)
    return (context, keys.reshape(total_tokens, inner), values.reshape(total_tokens, inner))


def expert_apply(picked, gate_w, up_w, down_w):
    gate_part = jnp.dot(picked, gate_w, preferred_element_type=jnp.float32)
    upward = jnp.dot(picked, up_w, preferred_element_type=jnp.float32)
    hidden = (jax.nn.silu(gate_part) * upward).astype(jnp.bfloat16)
    return jnp.dot(hidden, down_w, preferred_element_type=jnp.float32).astype(jnp.bfloat16)


def ring_reduce_scatter(partial, groups):
    ring = groups // 4
    rows = partial.shape[0] // groups
    width = partial.shape[1]
    me = lax.axis_index("tensor")
    y = me // 4
    side = me // 2 % 2
    core = me % 2
    blocks = partial.reshape(ring, 2, 2, rows, width)
    core_pairs = [(t, t ^ 1) for t in range(groups)]
    keep = lax.dynamic_index_in_dim(blocks, core, axis=2, keepdims=False)
    give = lax.dynamic_index_in_dim(blocks, 1 - core, axis=2, keepdims=False)
    got = lax.ppermute(give, "tensor", core_pairs)
    summed = keep.astype(jnp.float32) + got.astype(jnp.float32)
    half = width // 2
    forward_part = summed[..., :half]
    backward_part = summed[..., half:]
    forward_pairs = [(t, (t // 4 + 1) % ring * 4 + t % 4) for t in range(groups)]
    backward_pairs = [(t, (t // 4 + ring - 1) % ring * 4 + t % 4) for t in range(groups)]
    carry_f = lax.dynamic_index_in_dim(forward_part, (y + ring - 1) % ring, 0, False)
    carry_b = lax.dynamic_index_in_dim(backward_part, (y + 1) % ring, 0, False)
    carry_f = carry_f.astype(jnp.bfloat16)
    carry_b = carry_b.astype(jnp.bfloat16)
    for step in range(ring - 1):
        recv_f = lax.ppermute(carry_f, "tensor", forward_pairs)
        recv_b = lax.ppermute(carry_b, "tensor", backward_pairs)
        index_f = (y + 2 * ring - step - 2) % ring
        index_b = (y + step + 2) % ring
        acc_f = recv_f.astype(jnp.float32) + lax.dynamic_index_in_dim(
            forward_part, index_f, 0, False
        )
        acc_b = recv_b.astype(jnp.float32) + lax.dynamic_index_in_dim(
            backward_part, index_b, 0, False
        )
        carry_f = acc_f.astype(jnp.bfloat16)
        carry_b = acc_b.astype(jnp.bfloat16)
    mine = jnp.concatenate([acc_f, acc_b], axis=-1)
    side_pairs = [(t, t ^ 2) for t in range(groups)]
    keep_side = lax.dynamic_index_in_dim(mine, side, 0, False)
    give_side = lax.dynamic_index_in_dim(mine, 1 - side, 0, False).astype(jnp.bfloat16)
    got_side = lax.ppermute(give_side, "tensor", side_pairs)
    return keep_side + got_side.astype(jnp.float32)


def shards(
    tokens,
    segment_ids,
    attention_gain,
    query_weight,
    key_weight,
    value_weight,
    output_weight,
    ffn_gain,
    shared_gate,
    shared_up,
    shared_down,
    expert_gate,
    expert_up,
    expert_down,
    expert_ids,
    gate_weights,
    page_table,
):
    tok_dev = tokens.shape[0]
    groups = lax.axis_size("tensor")
    position = lax.axis_index("tensor")
    inner = query_weight.shape[1]
    head_count = inner // HD
    model_width = tokens.shape[1]
    projection = jnp.concatenate([query_weight, key_weight, value_weight], axis=1)
    normed_all = lax.all_gather(rms_scale(tokens, attention_gain), "tensor", axis=0, tiled=True)
    out_weight_all = lax.all_gather(output_weight, "tensor", axis=0, tiled=True)
    projected = lax.map(
        lambda rows: jnp.dot(rows, projection, preferred_element_type=jnp.float32).astype(
            jnp.bfloat16
        ),
        normed_all.reshape(4, -1, normed_all.shape[1]),
    ).reshape(normed_all.shape[0], -1)
    context, keys, values = attend(projected, segment_ids, head_count)
    cache = jnp.stack([keys, values]).reshape(2, -1, PAGE, inner)
    kv_pages = jnp.zeros_like(cache).at[:, page_table].set(cache)
    received = lax.all_to_all(
        context.reshape(groups, tok_dev, inner), "tensor", split_axis=0, concat_axis=0, tiled=True
    )
    context_rows = received.transpose(1, 0, 2).reshape(tok_dev, groups * inner)
    attention = jnp.dot(context_rows, out_weight_all, preferred_element_type=jnp.float32)
    residual = (tokens.astype(jnp.float32) + attention).astype(jnp.bfloat16)
    normed_ffn = rms_scale(residual, ffn_gain)
    pieces = 2
    piece_width = model_width // pieces
    normed_stream = lax.all_gather(normed_ffn, "tensor", axis=0, tiled=True)
    local_experts = expert_gate.shape[0]
    expert_count = local_experts * groups
    capacity = tok_dev * TOP // expert_count + tok_dev // 8
    id_blocks = expert_ids.reshape(groups, tok_dev, -1)
    gate_blocks = gate_weights.reshape(groups, tok_dev, -1)
    slots = jnp.arange(capacity, dtype=jnp.int32)
    onehots = []
    weights = []
    for local in range(local_experts):
        expert = position * local_experts + local
        chosen = id_blocks == expert
        hits = jnp.sum(chosen.astype(jnp.int32), axis=2)
        weights.append(jnp.sum(jnp.where(chosen, gate_blocks, 0.0), axis=2))
        rank = jnp.cumsum(hits, axis=1) - hits
        onehots.append(
            ((hits[:, None, :] > 0) & (rank[:, None, :] == slots[None, :, None])).astype(
                jnp.bfloat16
            )
        )
    shared_columns = jnp.concatenate([shared_gate, shared_up], axis=1)
    shared_width = shared_gate.shape[1]
    joined = jnp.dot(normed_stream, shared_columns, preferred_element_type=jnp.float32)
    token_blocks = normed_stream.reshape(groups, tok_dev, model_width)
    expert_gate_parts = []
    expert_up_parts = []
    for local in range(local_experts):
        picked = (
            jnp.einsum(
                "bst,btd->bsd", onehots[local], token_blocks, preferred_element_type=jnp.float32
            )
            .astype(jnp.bfloat16)
            .reshape(-1, model_width)
        )
        expert_gate_parts.append(
            jnp.dot(picked, expert_gate[local], preferred_element_type=jnp.float32)
        )
        expert_up_parts.append(
            jnp.dot(picked, expert_up[local], preferred_element_type=jnp.float32)
        )
    hidden_all = (jax.nn.silu(joined[:, :shared_width]) * joined[:, shared_width:]).astype(
        jnp.bfloat16
    )
    expert_hidden = [
        (jax.nn.silu(expert_gate_parts[local]) * expert_up_parts[local]).astype(jnp.bfloat16)
        for local in range(local_experts)
    ]
    outs = []
    for k in range(pieces):
        columns = slice(k * piece_width, (k + 1) * piece_width)
        term = jnp.dot(hidden_all, shared_down[:, columns], preferred_element_type=jnp.float32)
        for local in range(local_experts):
            rows = jnp.dot(
                expert_hidden[local],
                expert_down[local][:, columns],
                preferred_element_type=jnp.float32,
            ).astype(jnp.bfloat16)
            back = jnp.einsum(
                "bst,bsd->btd",
                onehots[local],
                rows.reshape(groups, capacity, piece_width),
                preferred_element_type=jnp.float32,
            ).astype(jnp.bfloat16)
            term = term + weights[local].reshape(-1, 1) * back.reshape(-1, piece_width).astype(
                jnp.float32
            )
        outs.append(ring_reduce_scatter(term.astype(jnp.bfloat16), groups))
    ffn_out = jnp.concatenate(outs, axis=1)
    layer_out = (residual.astype(jnp.float32) + ffn_out).astype(jnp.bfloat16)
    return (layer_out, kv_pages)


def solution(mesh):
    placed = (
        P(("dp", "tensor"), None),
        P("dp"),
        P(),
        P(None, "tensor"),
        P(None, "tensor"),
        P(None, "tensor"),
        P("tensor", None),
        P(),
        P(None, "tensor"),
        P(None, "tensor"),
        P("tensor", None),
        P("tensor", None, None),
        P("tensor", None, None),
        P("tensor", None, None),
        P("dp", None),
        P("dp", None),
        P("dp"),
    )
    return jax.shard_map(
        shards,
        mesh=mesh,
        in_specs=placed,
        out_specs=(P(("dp", "tensor"), None), P(None, "dp", None, "tensor")),
        check_vma=False,
    )
```

profile of v0, /device:TPU:0, one launch (start us, length us, event | category | flops | bytes accessed | tf_op | source)
XLA Modules:
  0.0 287.7 jit_solution(262670037977427516)
XLA Ops:
  12.9 52.3 %all-gather.4.cloned.1.call-done = bf16[2048,2048]{1,0:T(8,128)(2,1)} async-done(((bf16[128,2048]{1,0:T(8,128)(2,1)}), bf16[2048,2048]{1,0:T(8,128)(2,1)}) %all-gather.4.cloned.1.call-update) | async-done | bytes 8388624 | tf_op jit(solution)/shard_map/all_gather | solution.py:126
  65.2 14.6 %while.21 = (s32[]{:T(128)}, bf16[4,512,384]{2,1,0:T(8,128)(2,1)}, bf16[4,512,2048]{2,1,0:T(8,128)(2,1)}, bf16[2048,384]{1,0:T(8,128)(2,1)S(1)}, s32[]{:T(128)}) while((s32[]{:T(128)}, bf16[4,512,384]{2,1,0:T(8,128)(2,1)}, bf16[4,512,2048]{2,1,0:T(8,128)(2,1)}, bf16[2048,384]{1,0:T(8,128)(2,1)S(1)}, s32[]{:T(128)}) %tuple.62), condition=%wide.region_2.3_spmd, body=%wide.region_1.2_spmd.sunk | while | flops 805502976 | bytes 4064325 | solution.py:128
  65.2 3.6 %fusion.120 = bf16[4,512,384]{2,1,0:T(8,128)(2,1)} fusion(bf16[4,512,384]{2,1,0:T(8,128)(2,1)} %get-tuple-element.199, s32[]{:T(128)S(6)} %copy.34, bf16[2048,384]{1,0:T(8,128)(2,1)S(1)} %get-tuple-element.206, bf16[4,512,2048]{2,1,0:T(8,128)(2,1)} %get-tuple-element.205), kind=kOutput, calls=%fused_computation.7.clone.1 | convolution fusion | flops 805502976 | bytes 4064256 | tf_op jit(solution)/shard_map/while/body/eval_jaxpr/dot_general | solution.py:129
  68.8 3.6 %fusion.120 = bf16[4,512,384]{2,1,0:T(8,128)(2,1)} fusion(bf16[4,512,384]{2,1,0:T(8,128)(2,1)} %get-tuple-element.199, s32[]{:T(128)S(6)} %copy.34, bf16[2048,384]{1,0:T(8,128)(2,1)S(1)} %get-tuple-element.206, bf16[4,512,2048]{2,1,0:T(8,128)(2,1)} %get-tuple-element.205), kind=kOutput, calls=%fused_computation.7.clone.1 | convolution fusion | flops 805502976 | bytes 4064256 | tf_op jit(solution)/shard_map/while/body/eval_jaxpr/dot_general | solution.py:129
  72.4 3.6 %fusion.120 = bf16[4,512,384]{2,1,0:T(8,128)(2,1)} fusion(bf16[4,512,384]{2,1,0:T(8,128)(2,1)} %get-tuple-element.199, s32[]{:T(128)S(6)} %copy.34, bf16[2048,384]{1,0:T(8,128)(2,1)S(1)} %get-tuple-element.206, bf16[4,512,2048]{2,1,0:T(8,128)(2,1)} %get-tuple-element.205), kind=kOutput, calls=%fused_computation.7.clone.1 | convolution fusion | flops 805502976 | bytes 4064256 | tf_op jit(solution)/shard_map/while/body/eval_jaxpr/dot_general | solution.py:129
  76.0 3.8 %fusion.120 = bf16[4,512,384]{2,1,0:T(8,128)(2,1)} fusion(bf16[4,512,384]{2,1,0:T(8,128)(2,1)} %get-tuple-element.199, s32[]{:T(128)S(6)} %copy.34, bf16[2048,384]{1,0:T(8,128)(2,1)S(1)} %get-tuple-element.206, bf16[4,512,2048]{2,1,0:T(8,128)(2,1)} %get-tuple-element.205), kind=kOutput, calls=%fused_computation.7.clone.1 | convolution fusion | flops 805502976 | bytes 4064256 | tf_op jit(solution)/shard_map/while/body/eval_jaxpr/dot_general | solution.py:129
  82.5 23.1 %while.22 = (s32[]{:T(128)}, bf16[4,512,1,128]{3,1,2,0:T(8,128)(2,1)S(1)}, s32[4]{0:T(128)S(1)}, s32[2048]{0:T(1024)S(1)}, bf16[2048,1,128]{2,0,1:T(8,128)(2,1)S...) while((s32[]{:T(128)}, ...), condition=%wide.region_6.7_spmd.clone, body=%wide.region_3.6_spmd.clone.sunk | while | flops 548470272 | bytes 13922475 | solution.py:45
  105.6 20.5 %all_to_all.5 = bf16[16,128,128]{2,1,0:T(8,128)(2,1)S(1)} all-to-all(bf16[16,128,128]{2,1,0:T(8,128)(2,1)S(1)} %bitcast.200), channel_id=1, replica_groups=mesh['dp'=8,'tensor'=16] {'tensor'}, dimensions={0} | all-to-all | bytes 1048576 | tf_op jit(solution)/shard_map/all_to_all | solution.py:137
  126.4 4.8 %multiply_reduce_fusion = (f32[128]{0:T(128)S(1)}, f32[128,2048]{1,0:T(8,128)S(1)}) fusion(bf16[128,2048]{0,1:T(8,128)(2,1)S(1)} %bitcast.193, bf16[2048,2048]{1,0:T(8,128)(2,1)} %all-gather.6.cloned.1.call-done, bf16[128,2048]{1,0:T(8,128)(2,1)S(1)} %copy-done), kind=kOutput, calls=%fused_computation.76 | convolution fusion | flops 1075314560 | bytes 10486272 | tf_op jit(solution)/shard_map/dot_general | solution.py:141
  132.7 52.0 %all-gather.8.cloned.1.call-done = bf16[2048,2048]{1,0:T(8,128)(2,1)} async-done(((bf16[128,2048]{1,0:T(8,128)(2,1)}), bf16[2048,2048]{1,0:T(8,128)(2,1)}) %all-gather.8.cloned.1.call-update) | async-done | bytes 8388624 | tf_op jit(solution)/shard_map/all_gather | solution.py:146
  184.7 4.8 %convolution_convert_fusion = bf16[16,64,2048]{2,1,0:T(8,128)(2,1)S(1)} fusion(bf16[16,128,2048]{2,1,0:T(8,128)(2,1)} %bitcast.182, s32[16,128]{1,0:T(8,128)S(1)} %bitcast_subtract_fusion, pred[16,128]{1,0:T(8,128)(4,1)S(1)} %broadcast_compare_fusion.1), kind=kOutput, calls=%fused_computation.38 | convolution fusion | flops 539230208 | bytes 12593152 | tf_op jit(solution)/shard_map/bst,btd->bsd/dot_general | solution.py:174
  189.5 9.4 %fusion.32 = f32[1024,1408]{1,0:T(8,128)S(1)} fusion(bf16[1024,2048]{1,0:T(8,128)(2,1)S(1)} %bitcast.185, bf16[1,2048,1408]{2,1,0:T(8,128)(2,1)} %param.32), kind=kOutput, calls=%fused_computation.33 | convolution fusion | flops 5905580032 | bytes 15728640 | tf_op jit(solution)/shard_map/dot_general | solution.py:181
  198.9 7.0 %multiply_convert_fusion = bf16[1024,1408]{1,0:T(8,128)(2,1)S(1)} fusion(f32[1024,1408]{1,0:T(8,128)S(1)} %fusion.32, bf16[1024,2048]{1,0:T(8,128)(2,1)S(1)} %bitcast.186, bf16[1,2048,1408]{2,1,0:T(8,128)(2,1)S(1)} %bitcast.204), kind=kOutput, calls=%fused_computation.35 | convolution fusion | flops 5914230784 | bytes 18612224 | tf_op jit(solution)/shard_map/dot_general | solution.py:184
  206.0 3.6 %fusion.45 = bf16[1024,1024]{1,0:T(8,128)(2,1)S(1)} fusion(bf16[1024,1408]{1,0:T(8,128)(2,1)S(1)} %multiply_convert_fusion, bf16[1408,2048]{1,0:T(8,128)(2,1)S(1)} %bitcast.207), kind=kOutput, calls=%fused_computation.51 | convolution fusion | flops 2953838592 | bytes 7864320 | tf_op jit(solution)/shard_map/dot_general | solution.py:198
  209.7 3.9 %fusion.42 = bf16[1024,1024]{1,0:T(8,128)(2,1)S(1)} fusion(bf16[1024,1408]{1,0:T(8,128)(2,1)S(1)} %multiply_convert_fusion, bf16[1408,2048]{1,0:T(8,128)(2,1)S(1)} %bitcast.208), kind=kOutput, calls=%fused_computation.50 | convolution fusion | flops 2953838592 | bytes 7864320 | tf_op jit(solution)/shard_map/dot_general | solution.py:198
  213.6 3.2 %fusion.49 = f32[2048,352]{0,1:T(8,128)S(1)} fusion(bf16[2048,2048]{1,0:T(8,128)(2,1)S(1)} %bitcast.184, bf16[2048,176]{0,1:T(8,128)(2,1)S(1)} %copy-done.10, bf16[2048,176]{0,1:T(8,128)(2,1)S(1)} %copy-done.11), kind=kOutput, calls=%fused_computation.57 | convolution fusion | flops 2955673600 | bytes 12713984 | tf_op jit(solution)/shard_map/dot_general | solution.py:168
  227.8 3.2 %convert_add_fusion = f32[4,2,128,1024]{3,2,1,0:T(8,128)S(1)} fusion(bf16[4,2,128,1024]{3,2,1,0:T(8,128)(2,1)} %collective-permute-done.8, bf16[4,2,2,128,1024]{4,3,2,1,0:T(8,128)(2,1)} %bitcast.192, s32[]{:T(128)S(6)} %select_n.134), kind=kLoop, calls=%fused_computation.36 | loop fusion | flops 3145728 | bytes 8388612 | tf_op jit(solution)/shard_map/add | solution.py:69
  238.9 3.0 %collective-permute-start.4 = (bf16[2,128,512]{2,1,0:T(8,128)(2,1)S(1)}, bf16[2,128,512]{2,1,0:T(8,128)(2,1)S(1)}, u32[]{:S(2)}, u32[]{:S(2)}) collective-permute-start(bf16[2,128,512]{2,1,0:T(8,128)(2,1)S(1)} %fusion.82), channel_id=1, source_target_pairs={{0,12},{1,13},{2,14},{3,15},{4,0},{5,1},{6,2},{7,3},{8,4},{9,5},{1... | collective-permute-start | bytes 786440 | tf_op jit(solution)/shard_map/ppermute | solution.py:81
  242.3 3.1 %collective-permute-start.13 = (bf16[2,128,512]{2,1,0:T(8,128)(2,1)S(1)}, bf16[2,128,512]{2,1,0:T(8,128)(2,1)S(1)}, u32[]{:S(2)}, u32[]{:S(2)}) collective-permute-start(bf16[2,128,512]{2,1,0:T(8,128)(2,1)S(1)} %fusion.68), channel_id=1, source_target_pairs={{0,12},{1,13},{2,14},{3,15},{4,0},{5,1},{6,2},{7,3},{8,4},{9,5},{1... | collective-permute-start | bytes 786440 | tf_op jit(solution)/shard_map/ppermute | solution.py:81
  245.4 3.7 %collective-permute-done.1 = bf16[2,128,512]{2,1,0:T(8,128)(2,1)S(1)} collective-permute-done((bf16[2,128,512]{2,1,0:T(8,128)(2,1)S(1)}, bf16[2,128,512]{2,1,0:T(8,128)(2,1)S(1)}, u32[]{:S(2)}, u32[]{:S(2)}) %collective-permute-start.1) | collective-permute-done | bytes 262176 | tf_op jit(solution)/shard_map/ppermute | solution.py:80
  249.3 3.3 %collective-permute-start.5 = (bf16[2,128,512]{2,1,0:T(8,128)(2,1)S(1)}, bf16[2,128,512]{2,1,0:T(8,128)(2,1)S(1)}, u32[]{:S(2)}, u32[]{:S(2)}) collective-permute-start(bf16[2,128,512]{2,1,0:T(8,128)(2,1)S(1)} %fusion.72), channel_id=1, source_target_pairs={{0,12},{1,13},{2,14},{3,15},{4,0},{5,1},{6,2},{7,3},{8,4},{9,5},{1... | collective-permute-start | bytes 786440 | tf_op jit(solution)/shard_map/ppermute | solution.py:81
  254.9 3.3 %collective-permute-start.14 = (bf16[2,128,512]{2,1,0:T(8,128)(2,1)S(1)}, bf16[2,128,512]{2,1,0:T(8,128)(2,1)S(1)}, u32[]{:S(2)}, u32[]{:S(2)}) collective-permute-start(bf16[2,128,512]{2,1,0:T(8,128)(2,1)S(1)} %fusion.67), channel_id=1, source_target_pairs={{0,12},{1,13},{2,14},{3,15},{4,0},{5,1},{6,2},{7,3},{8,4},{9,5},{1... | collective-permute-start | bytes 786440 | tf_op jit(solution)/shard_map/ppermute | solution.py:81
  260.6 3.3 %collective-permute-start.6 = (bf16[2,128,512]{2,1,0:T(8,128)(2,1)S(1)}, bf16[2,128,512]{2,1,0:T(8,128)(2,1)S(1)}, u32[]{:S(2)}, u32[]{:S(2)}) collective-permute-start(bf16[2,128,512]{2,1,0:T(8,128)(2,1)S(1)} %fusion.71), channel_id=1, source_target_pairs={{0,12},{1,13},{2,14},{3,15},{4,0},{5,1},{6,2},{7,3},{8,4},{9,5},{1... | collective-permute-start | bytes 786440 | tf_op jit(solution)/shard_map/ppermute | solution.py:81
  274.8 3.4 %scatter_fusion = bf16[2,16,128,128]{3,2,1,0:T(8,128)(2,1)} fusion(bf16[2,16,128,128]{3,2,1,0:T(8,128)(2,1)} %broadcast_in_dim.45, s32[16]{0:T(128)S(1)} %compare_select_fusion, bf16[16,2,128,128]{3,2,1,0:T(8,128)(2,1)} %maximum_bitcast_fusion), kind=kCustom, calls=%fused_computation | custom fusion | bytes 3145792 | tf_op jit(solution)/shard_map/scatter | solution.py:136
  (150 shorter events, 64.4 us)
Async XLA Ops:
  7.2 58.1 %all-gather.4.cloned.1.call-start = ((), (), s32[]{:S(2)}) async-start(), calls=%async_computation.1 | async-start | bytes 8912896 | tf_op jit(solution)/shard_map/all_gather | solution.py:126
  10.5 115.9 %all-gather.6.cloned.1.call-start = ((), (), s32[]{:S(2)}) async-start(), calls=%async_computation.2 | async-start | bytes 8912896 | tf_op jit(solution)/shard_map/all_gather | solution.py:127
  11.3 173.4 %all-gather.8.cloned.1.call-start = ((), (), s32[]{:S(2)}) async-start(), calls=%async_computation.3 | async-start | bytes 8912896 | tf_op jit(solution)/shard_map/all_gather | solution.py:146
  82.5 43.9 %copy-start = (bf16[128,2048]{1,0:T(8,128)(2,1)S(1)}, bf16[128,2048]{1,0:T(8,128)(2,1)}, u32[]{:S(2)}) copy-start(bf16[128,2048]{1,0:T(8,128)(2,1)} %param.21) | copy-start | bytes 1572868
  184.7 14.2 %slice-start.2 = ((s8[5767168]{0:T(1024)(128)(4,1)}), s8[4194304]{0:T(1024)(128)(4,1)S(1)}, s32[]{:S(2)}) async-start(s8[5767168]{0:T(1024)(128)(4,1)} %bitcast.203), calls=%async_computation.6 | async-start | bytes 8388608
  189.5 16.5 %slice-start.4 = ((s8[5767168]{0:T(1024)(128)(4,1)}), s8[4194304]{0:T(1024)(128)(4,1)S(1)}, s32[]{:S(2)}) async-start(s8[5767168]{0:T(1024)(128)(4,1)} %bitcast.205), calls=%async_computation.8 | async-start | bytes 8388608
  222.0 5.8 %collective-permute-start.8 = (bf16[4,2,128,1024]{3,2,1,0:T(8,128)(2,1)}, bf16[4,2,128,1024]{3,2,1,0:T(8,128)(2,1)}, u32[]{:S(2)}, u32[]{:S(2)}) collective-permute-start(bf16[4,2,128,1024]{3,2,1,0:T(8,128)(2,1)} %dynamic-slice_bitcast_fusion), channel_id=1, source_target_pairs={{0,1},{1,0},{2,3},{3,2},{4,5},{5,4},{6,7},{7,6},{8,9},{9,8},{10,11... | collective-permute-start | bytes 6291464 | tf_op jit(solution)/shard_map/ppermute | solution.py:68
  227.4 7.6 %collective-permute-start = (bf16[4,2,128,1024]{3,2,1,0:T(8,128)(2,1)S(1)}, bf16[4,2,128,1024]{3,2,1,0:T(8,128)(2,1)}, u32[]{:S(2)}, u32[]{:S(2)}) collective-permute-start(bf16[4,2,128,1024]{3,2,1,0:T(8,128)(2,1)S(1)} %dynamic-slice_bitcast_fusion.1), channel_id=1, source_target_pairs={{0,1},{1,0},{2,3},{3,2},{4,5},{5,4},{6,7},{7,6},{8,9},{9,8},{10,11... | collective-permute-start | bytes 6291464 | tf_op jit(solution)/shard_map/ppermute | solution.py:68
  231.7 10.2 %collective-permute-start.9 = (bf16[2,128,512]{2,1,0:T(8,128)(2,1)S(1)}, bf16[2,128,512]{2,1,0:T(8,128)(2,1)S(1)}, u32[]{:S(2)}, u32[]{:S(2)}) collective-permute-start(bf16[2,128,512]{2,1,0:T(8,128)(2,1)S(1)} %fusion.83), channel_id=1, source_target_pairs={{0,4},{1,5},{2,6},{3,7},{4,8},{5,9},{6,10},{7,11},{8,12},{9,13},{1... | collective-permute-start | bytes 786440 | tf_op jit(solution)/shard_map/ppermute | solution.py:80
  233.2 9.0 %collective-permute-start.12 = (bf16[2,128,512]{2,1,0:T(8,128)(2,1)S(1)}, bf16[2,128,512]{2,1,0:T(8,128)(2,1)S(1)}, u32[]{:S(2)}, u32[]{:S(2)}) collective-permute-start(bf16[2,128,512]{2,1,0:T(8,128)(2,1)S(1)} %fusion.84), channel_id=1, source_target_pairs={{0,12},{1,13},{2,14},{3,15},{4,0},{5,1},{6,2},{7,3},{8,4},{9,5},{1... | collective-permute-start | bytes 786440 | tf_op jit(solution)/shard_map/ppermute | solution.py:81
  238.3 10.8 %collective-permute-start.1 = (bf16[2,128,512]{2,1,0:T(8,128)(2,1)S(1)}, bf16[2,128,512]{2,1,0:T(8,128)(2,1)S(1)}, u32[]{:S(2)}, u32[]{:S(2)}) collective-permute-start(bf16[2,128,512]{2,1,0:T(8,128)(2,1)S(1)} %fusion.81), channel_id=1, source_target_pairs={{0,4},{1,5},{2,6},{3,7},{4,8},{5,9},{6,10},{7,11},{8,12},{9,13},{1... | collective-permute-start | bytes 786440 | tf_op jit(solution)/shard_map/ppermute | solution.py:80
  238.9 10.3 %collective-permute-start.4 = (bf16[2,128,512]{2,1,0:T(8,128)(2,1)S(1)}, bf16[2,128,512]{2,1,0:T(8,128)(2,1)S(1)}, u32[]{:S(2)}, u32[]{:S(2)}) collective-permute-start(bf16[2,128,512]{2,1,0:T(8,128)(2,1)S(1)} %fusion.82), channel_id=1, source_target_pairs={{0,12},{1,13},{2,14},{3,15},{4,0},{5,1},{6,2},{7,3},{8,4},{9,5},{1... | collective-permute-start | bytes 786440 | tf_op jit(solution)/shard_map/ppermute | solution.py:81
  242.0 12.7 %collective-permute-start.10 = (bf16[2,128,512]{2,1,0:T(8,128)(2,1)S(1)}, bf16[2,128,512]{2,1,0:T(8,128)(2,1)S(1)}, u32[]{:S(2)}, u32[]{:S(2)}) collective-permute-start(bf16[2,128,512]{2,1,0:T(8,128)(2,1)S(1)} %fusion.70), channel_id=1, source_target_pairs={{0,4},{1,5},{2,6},{3,7},{4,8},{5,9},{6,10},{7,11},{8,12},{9,13},{1... | collective-permute-start | bytes 786440 | tf_op jit(solution)/shard_map/ppermute | solution.py:80
  242.3 12.5 %collective-permute-start.13 = (bf16[2,128,512]{2,1,0:T(8,128)(2,1)S(1)}, bf16[2,128,512]{2,1,0:T(8,128)(2,1)S(1)}, u32[]{:S(2)}, u32[]{:S(2)}) collective-permute-start(bf16[2,128,512]{2,1,0:T(8,128)(2,1)S(1)} %fusion.68), channel_id=1, source_target_pairs={{0,12},{1,13},{2,14},{3,15},{4,0},{5,1},{6,2},{7,3},{8,4},{9,5},{1... | collective-permute-start | bytes 786440 | tf_op jit(solution)/shard_map/ppermute | solution.py:81
  249.1 11.2 %collective-permute-start.2 = (bf16[2,128,512]{2,1,0:T(8,128)(2,1)S(1)}, bf16[2,128,512]{2,1,0:T(8,128)(2,1)S(1)}, u32[]{:S(2)}, u32[]{:S(2)}) collective-permute-start(bf16[2,128,512]{2,1,0:T(8,128)(2,1)S(1)} %fusion.74), channel_id=1, source_target_pairs={{0,4},{1,5},{2,6},{3,7},{4,8},{5,9},{6,10},{7,11},{8,12},{9,13},{1... | collective-permute-start | bytes 786440 | tf_op jit(solution)/shard_map/ppermute | solution.py:80
  249.3 11.1 %collective-permute-start.5 = (bf16[2,128,512]{2,1,0:T(8,128)(2,1)S(1)}, bf16[2,128,512]{2,1,0:T(8,128)(2,1)S(1)}, u32[]{:S(2)}, u32[]{:S(2)}) collective-permute-start(bf16[2,128,512]{2,1,0:T(8,128)(2,1)S(1)} %fusion.72), channel_id=1, source_target_pairs={{0,12},{1,13},{2,14},{3,15},{4,0},{5,1},{6,2},{7,3},{8,4},{9,5},{1... | collective-permute-start | bytes 786440 | tf_op jit(solution)/shard_map/ppermute | solution.py:81
  254.8 11.2 %collective-permute-start.11 = (bf16[2,128,512]{2,1,0:T(8,128)(2,1)S(1)}, bf16[2,128,512]{2,1,0:T(8,128)(2,1)S(1)}, u32[]{:S(2)}, u32[]{:S(2)}) collective-permute-start(bf16[2,128,512]{2,1,0:T(8,128)(2,1)S(1)} %fusion.69), channel_id=1, source_target_pairs={{0,4},{1,5},{2,6},{3,7},{4,8},{5,9},{6,10},{7,11},{8,12},{9,13},{1... | collective-permute-start | bytes 786440 | tf_op jit(solution)/shard_map/ppermute | solution.py:80
  254.9 11.1 %collective-permute-start.14 = (bf16[2,128,512]{2,1,0:T(8,128)(2,1)S(1)}, bf16[2,128,512]{2,1,0:T(8,128)(2,1)S(1)}, u32[]{:S(2)}, u32[]{:S(2)}) collective-permute-start(bf16[2,128,512]{2,1,0:T(8,128)(2,1)S(1)} %fusion.67), channel_id=1, source_target_pairs={{0,12},{1,13},{2,14},{3,15},{4,0},{5,1},{6,2},{7,3},{8,4},{9,5},{1... | collective-permute-start | bytes 786440 | tf_op jit(solution)/shard_map/ppermute | solution.py:81
  260.4 9.8 %collective-permute-start.3 = (bf16[2,128,512]{2,1,0:T(8,128)(2,1)S(1)}, bf16[2,128,512]{2,1,0:T(8,128)(2,1)S(1)}, u32[]{:S(2)}, u32[]{:S(2)}) collective-permute-start(bf16[2,128,512]{2,1,0:T(8,128)(2,1)S(1)} %fusion.73), channel_id=1, source_target_pairs={{0,4},{1,5},{2,6},{3,7},{4,8},{5,9},{6,10},{7,11},{8,12},{9,13},{1... | collective-permute-start | bytes 786440 | tf_op jit(solution)/shard_map/ppermute | solution.py:80
  260.5 12.0 %copy-start.4 = (bf16[2048,128]{1,0:T(8,128)(2,1)S(1)}, bf16[2048,128]{1,0:T(8,128)(2,1)}, u32[]{:S(2)}) copy-start(bf16[2048,128]{1,0:T(8,128)(2,1)} %get-tuple-element.114) | copy-start | bytes 1572868
  260.6 12.0 %copy-start.5 = (bf16[2048,128]{1,0:T(8,128)(2,1)S(1)}, bf16[2048,128]{1,0:T(8,128)(2,1)}, u32[]{:S(2)}) copy-start(bf16[2048,128]{1,0:T(8,128)(2,1)} %get-tuple-element.117) | copy-start | bytes 1572868
  260.6 9.7 %collective-permute-start.6 = (bf16[2,128,512]{2,1,0:T(8,128)(2,1)S(1)}, bf16[2,128,512]{2,1,0:T(8,128)(2,1)S(1)}, u32[]{:S(2)}, u32[]{:S(2)}) collective-permute-start(bf16[2,128,512]{2,1,0:T(8,128)(2,1)S(1)} %fusion.71), channel_id=1, source_target_pairs={{0,12},{1,13},{2,14},{3,15},{4,0},{5,1},{6,2},{7,3},{8,4},{9,5},{1... | collective-permute-start | bytes 786440 | tf_op jit(solution)/shard_map/ppermute | solution.py:81
  266.1 12.1 %collective-permute-start.15 = (bf16[128,1024]{1,0:T(8,128)(2,1)S(1)}, bf16[128,1024]{1,0:T(8,128)(2,1)}, u32[]{:S(2)}, u32[]{:S(2)}) collective-permute-start(bf16[128,1024]{1,0:T(8,128)(2,1)S(1)} %fusion.86), channel_id=1, source_target_pairs={{0,2},{1,3},{2,0},{3,1},{4,6},{5,7},{6,4},{7,5},{8,10},{9,11},{10,... | collective-permute-start | bytes 786440 | tf_op jit(solution)/shard_map/ppermute | solution.py:96
  271.1 8.1 %collective-permute-start.7 = (bf16[128,1024]{1,0:T(8,128)(2,1)}, bf16[128,1024]{1,0:T(8,128)(2,1)}, u32[]{:S(2)}, u32[]{:S(2)}) collective-permute-start(bf16[128,1024]{1,0:T(8,128)(2,1)} %fusion.85), channel_id=1, source_target_pairs={{0,2},{1,3},{2,0},{3,1},{4,6},{5,7},{6,4},{7,5},{8,10},{9,11},{10,... | collective-permute-start | bytes 786440 | tf_op jit(solution)/shard_map/ppermute | solution.py:96
  (15 other events, 68.7 us)
Sparse Core Ops, SparseCore 0:
  10.6 54.5 all-gather.3
  66.9 58.6 all-gather.5
  132.4 52.2 all-gather.7
where the time goes:
time: 288 us
  waiting for transfers between devices  118 us (41%)
  matrix products  66 us (23%)
  starting transfers between devices  23.9 us (8%)
  other arithmetic  23 us (8%)
  blocking collectives  20.5 us (7%)
  local copies, waits for them, and re-layouts  15.6 us (5%)
  between operations  14.4 us (5%)
  loops' own time  6.69 us (2%)
    all_gather x1, waiting for transfers between devices, shards(): lax.all_gather(rms_scale(tokens, attention_gain), 'tensor', axis=0, tiled...  52.3 us
    all_gather x1, waiting for transfers between devices, shards(): normed_stream = lax.all_gather(normed_ffn, 'tensor', axis=0, tiled=True)  52 us
    all_to_all x1, blocking collectives, shards(): lax.all_to_all(context.reshape(groups, tok_dev, inner), 'tensor', split_a...  20.5 us
    ppermute x6, starting transfers between devices, ring_reduce_scatter(): recv_b = lax.ppermute(carry_b, 'tensor', backward_pairs)  17.7 us
    dot_general x4, matrix products, shards(): jnp.dot(rows, projection, preferred_element_type=jnp.float32)  14.6 us
    ppermute x6, waiting for transfers between devices, ring_reduce_scatter(): recv_f = lax.ppermute(carry_f, 'tensor', forward_pairs)  12.5 us
    dot_general x1, matrix products, shards(): jnp.dot(picked, expert_gate[local], preferred_element_type=jnp.float32)  9.35 us
    dot_general x2, matrix products, shards(): jnp.dot(expert_hidden[local], expert_down[local][:, columns], preferred_e...  7.49 us
  transfers between devices with their start and end apart: 19, of which 7 were waited for; matrix products, arithmetic and copies ran while one was open for 19% of the time, Pallas kernels for 0%

commit v1 on v0

--- a/solution.py
+++ b/solution.py
@@ -143,7 +143,8 @@
     normed_ffn = rms_scale(residual, ffn_gain)
     pieces = 2
     piece_width = model_width // pieces
-    normed_stream = lax.all_gather(normed_ffn, "tensor", axis=0, tiled=True)
+    sent = jnp.stack([normed_ffn] * lax.axis_size("tensor"))
+    normed_stream = jnp.concatenate(lax.all_to_all(sent, "tensor", 0, 0), axis=0)
     local_experts = expert_gate.shape[0]
     expert_count = local_experts * groups
     capacity = tok_dev * TOP // expert_count + tok_dev // 8

time: 288 us -> 341 us (1.18)
  waiting for transfers between devices: 118 us -> 161 us
  local copies, waits for them, and re-layouts: 15.6 us -> 20.1 us
  starting transfers between devices: 23.9 us -> 27.4 us
    all_to_all x0 -> x1, waiting for transfers between devices: none -> 94.7 us  [shards(): lax.all_to_all(sent, 'tensor', 0, 0)]
    all_gather x1 -> x0, waiting for transfers between devices: 52 us -> none  [shards(): normed_stream = lax.all_gather(normed_ffn, 'tensor', axis=0, tiled=True)]
    all_to_all x0 -> x1, starting transfers between devices: none -> 5.07 us  [shards(): lax.all_to_all(sent, 'tensor', 0, 0)]
    another operation x0 -> x1, local copies, waits for them, and re-layouts: none -> 4.3 us  [shards(): sent = jnp.stack([normed_ffn] * lax.axis_size('tensor'))]
  transfers between devices with their start and end apart: 19 -> 19, of which waited for: 7 -> 7; matrix products, arithmetic and copies ran while one was open for 19% -> 16% of each run, Pallas kernels for 0% -> 0%
where the time goes in v1:
time: 341 us
  waiting for transfers between devices  161 us (47%)
  matrix products  68.5 us (20%)
  starting transfers between devices  27.4 us (8%)
  other arithmetic  22.5 us (7%)
  local copies, waits for them, and re-layouts  20.1 us (6%)
  blocking collectives  18.8 us (6%)
  between operations  14.7 us (4%)
  loops' own time  7.77 us (2%)
    all_to_all x1, waiting for transfers between devices, shards(): lax.all_to_all(sent, 'tensor', 0, 0)  94.7 us
    all_gather x1, waiting for transfers between devices, shards(): lax.all_gather(rms_scale(tokens, attention_gain), 'tensor', axis=0, tiled...  52.4 us
    ppermute x6, starting transfers between devices, ring_reduce_scatter(): recv_b = lax.ppermute(carry_b, 'tensor', backward_pairs)  19.4 us
    all_to_all x1, blocking collectives, shards(): lax.all_to_all(context.reshape(groups, tok_dev, inner), 'tensor', split_a...  18.8 us
    dot_general x4, matrix products, shards(): jnp.dot(rows, projection, preferred_element_type=jnp.float32)  14.7 us
    ppermute x6, waiting for transfers between devices, ring_reduce_scatter(): recv_f = lax.ppermute(carry_f, 'tensor', forward_pairs)  13 us
    dot_general x1, matrix products, shards(): jnp.dot(picked, expert_gate[local], preferred_element_type=jnp.float32)  9.37 us
    another operation x1, loops' own time, attend(): context = lax.map(one_block, starts).reshape(total_tokens, inner)  7.76 us
  transfers between devices with their start and end apart: 19, of which 7 were waited for; matrix products, arithmetic and copies ran while one was open for 16% of the time, Pallas kernels for 0%

profile of v1, /device:TPU:0, one launch (start us, length us, event | category | flops | bytes accessed | tf_op | source)
XLA Modules:
  0.0 340.6 jit_solution(13345252364971754919)
XLA Ops:
  12.9 52.4 %all-gather.3.cloned.1.call-done = bf16[2048,2048]{1,0:T(8,128)(2,1)} async-done(((bf16[128,2048]{1,0:T(8,128)(2,1)}), bf16[2048,2048]{1,0:T(8,128)(2,1)}) %all-gather.3.cloned.1.call-update) | async-done | bytes 8388624 | tf_op jit(solution)/shard_map/all_gather | solution.py:126
  65.2 14.7 %while.21 = (s32[]{:T(128)}, bf16[4,512,384]{2,1,0:T(8,128)(2,1)}, bf16[4,512,2048]{2,1,0:T(8,128)(2,1)}, bf16[2048,384]{1,0:T(8,128)(2,1)S(1)}, s32[]{:T(128)}) while((s32[]{:T(128)}, bf16[4,512,384]{2,1,0:T(8,128)(2,1)}, bf16[4,512,2048]{2,1,0:T(8,128)(2,1)}, bf16[2048,384]{1,0:T(8,128)(2,1)S(1)}, s32[]{:T(128)}) %tuple.60), condition=%wide.region_2.3_spmd, body=%wide.region_1.2_spmd.sunk | while | flops 805502976 | bytes 4064325 | solution.py:128
  65.2 3.6 %fusion.120 = bf16[4,512,384]{2,1,0:T(8,128)(2,1)} fusion(bf16[4,512,384]{2,1,0:T(8,128)(2,1)} %get-tuple-element.199, s32[]{:T(128)S(6)} %copy.34, bf16[2048,384]{1,0:T(8,128)(2,1)S(1)} %get-tuple-element.206, bf16[4,512,2048]{2,1,0:T(8,128)(2,1)} %get-tuple-element.205), kind=kOutput, calls=%fused_computation.7.clone.1 | convolution fusion | flops 805502976 | bytes 4064256 | tf_op jit(solution)/shard_map/while/body/eval_jaxpr/dot_general | solution.py:129
  68.8 3.6 %fusion.120 = bf16[4,512,384]{2,1,0:T(8,128)(2,1)} fusion(bf16[4,512,384]{2,1,0:T(8,128)(2,1)} %get-tuple-element.199, s32[]{:T(128)S(6)} %copy.34, bf16[2048,384]{1,0:T(8,128)(2,1)S(1)} %get-tuple-element.206, bf16[4,512,2048]{2,1,0:T(8,128)(2,1)} %get-tuple-element.205), kind=kOutput, calls=%fused_computation.7.clone.1 | convolution fusion | flops 805502976 | bytes 4064256 | tf_op jit(solution)/shard_map/while/body/eval_jaxpr/dot_general | solution.py:129
  72.4 3.6 %fusion.120 = bf16[4,512,384]{2,1,0:T(8,128)(2,1)} fusion(bf16[4,512,384]{2,1,0:T(8,128)(2,1)} %get-tuple-element.199, s32[]{:T(128)S(6)} %copy.34, bf16[2048,384]{1,0:T(8,128)(2,1)S(1)} %get-tuple-element.206, bf16[4,512,2048]{2,1,0:T(8,128)(2,1)} %get-tuple-element.205), kind=kOutput, calls=%fused_computation.7.clone.1 | convolution fusion | flops 805502976 | bytes 4064256 | tf_op jit(solution)/shard_map/while/body/eval_jaxpr/dot_general | solution.py:129
  76.0 3.9 %fusion.120 = bf16[4,512,384]{2,1,0:T(8,128)(2,1)} fusion(bf16[4,512,384]{2,1,0:T(8,128)(2,1)} %get-tuple-element.199, s32[]{:T(128)S(6)} %copy.34, bf16[2048,384]{1,0:T(8,128)(2,1)S(1)} %get-tuple-element.206, bf16[4,512,2048]{2,1,0:T(8,128)(2,1)} %get-tuple-element.205), kind=kOutput, calls=%fused_computation.7.clone.1 | convolution fusion | flops 805502976 | bytes 4064256 | tf_op jit(solution)/shard_map/while/body/eval_jaxpr/dot_general | solution.py:129
  82.5 24.7 %while.22 = (s32[]{:T(128)}, bf16[4,512,1,128]{3,1,2,0:T(8,128)(2,1)S(1)}, s32[4]{0:T(128)S(1)}, s32[2048]{0:T(1024)S(1)}, bf16[2048,1,128]{2,0,1:T(8,128)(2,1)S...) while((s32[]{:T(128)}, ...), condition=%wide.region_6.7_spmd.clone, body=%wide.region_3.6_spmd.clone.sunk | while | flops 548470272 | bytes 13922475 | solution.py:45
  107.3 18.8 %all_to_all.10 = bf16[16,128,128]{2,1,0:T(8,128)(2,1)S(1)} all-to-all(bf16[16,128,128]{2,1,0:T(8,128)(2,1)S(1)} %bitcast.197), channel_id=1, replica_groups=mesh['dp'=8,'tensor'=16] {'tensor'}, dimensions={0} | all-to-all | bytes 1048576 | tf_op jit(solution)/shard_map/all_to_all | solution.py:137
  126.4 4.7 %multiply_reduce_fusion = (f32[128]{0:T(128)S(1)}, f32[128,2048]{1,0:T(8,128)S(1)}) fusion(bf16[128,2048]{0,1:T(8,128)(2,1)S(1)} %bitcast.190, bf16[2048,2048]{1,0:T(8,128)(2,1)} %all-gather.5.cloned.1.call-done, bf16[128,2048]{1,0:T(8,128)(2,1)S(1)} %copy-done), kind=kOutput, calls=%fused_computation.76 | convolution fusion | flops 1075314560 | bytes 10486272 | tf_op jit(solution)/shard_map/dot_general | solution.py:141
  131.3 4.3 %stack.8 = bf16[16,128,2048]{2,1,0:T(8,128)(2,1)} broadcast(bf16[128,2048]{1,0:T(8,128)(2,1)S(1)} %multiply_convert_fusion.1), dimensions={1,2} | broadcast | bytes 8912896 | tf_op jit(solution)/shard_map/stack | solution.py:146
  135.6 5.1 %all-to-all-start.1 = ((bf16[16,128,2048]{2,1,0:T(8,128)(2,1)}), bf16[16,128,2048]{2,1,0:T(8,128)(2,1)}, u32[]{:S(2)}, u32[]{:S(2)}) async-start(bf16[16,128,2048]{2,1,0:T(8,128)(2,1)} %stack.8), calls=%async_computation.1 | async-start | bytes 16777216 | tf_op jit(solution)/shard_map/all_to_all | solution.py:147
  141.1 94.7 %all-to-all-done.1 = bf16[16,128,2048]{2,1,0:T(8,128)(2,1)} async-done(((bf16[16,128,2048]{2,1,0:T(8,128)(2,1)}), bf16[16,128,2048]{2,1,0:T(8,128)(2,1)}, u32[]{:S(2)}, u32[]{:S(2)}) %all-to-all-start.1) | async-done | bytes 8388640 | tf_op jit(solution)/shard_map/all_to_all | solution.py:147
  235.9 4.8 %convolution_convert_fusion = bf16[16,64,2048]{2,1,0:T(8,128)(2,1)S(1)} fusion(bf16[16,128,2048]{2,1,0:T(8,128)(2,1)} %all-to-all-done.1, s32[16,128]{1,0:T(8,128)S(1)} %bitcast_subtract_fusion, pred[16,128]{1,0:T(8,128)(4,1)S(1)} %broadcast_compare_fusion.1), kind=kOutput, calls=%fused_computation.38 | convolution fusion | flops 539230208 | bytes 12593152 | tf_op jit(solution)/shard_map/bst,btd->bsd/dot_general | solution.py:175
  240.7 9.4 %fusion.32 = f32[1024,1408]{1,0:T(8,128)S(1)} fusion(bf16[1024,2048]{1,0:T(8,128)(2,1)S(1)} %bitcast.182, bf16[1,2048,1408]{2,1,0:T(8,128)(2,1)} %param.32), kind=kOutput, calls=%fused_computation.33 | convolution fusion | flops 5905580032 | bytes 15728640 | tf_op jit(solution)/shard_map/dot_general | solution.py:182
  250.1 7.1 %multiply_convert_fusion = bf16[1024,1408]{1,0:T(8,128)(2,1)S(1)} fusion(f32[1024,1408]{1,0:T(8,128)S(1)} %fusion.32, bf16[1024,2048]{1,0:T(8,128)(2,1)S(1)} %bitcast.183, bf16[1,2048,1408]{2,1,0:T(8,128)(2,1)S(1)} %bitcast.201), kind=kOutput, calls=%fused_computation.35 | convolution fusion | flops 5914230784 | bytes 18612224 | tf_op jit(solution)/shard_map/dot_general | solution.py:185
  257.2 3.6 %fusion.45 = bf16[1024,1024]{1,0:T(8,128)(2,1)S(1)} fusion(bf16[1024,1408]{1,0:T(8,128)(2,1)S(1)} %multiply_convert_fusion, bf16[1408,2048]{1,0:T(8,128)(2,1)S(1)} %bitcast.204), kind=kOutput, calls=%fused_computation.51 | convolution fusion | flops 2953838592 | bytes 7864320 | tf_op jit(solution)/shard_map/dot_general | solution.py:199
  260.9 3.6 %fusion.42 = bf16[1024,1024]{1,0:T(8,128)(2,1)S(1)} fusion(bf16[1024,1408]{1,0:T(8,128)(2,1)S(1)} %multiply_convert_fusion, bf16[1408,2048]{1,0:T(8,128)(2,1)S(1)} %bitcast.205), kind=kOutput, calls=%fused_computation.50 | convolution fusion | flops 2953838592 | bytes 7864320 | tf_op jit(solution)/shard_map/dot_general | solution.py:199
  264.5 5.8 %fusion.49 = f32[2048,352]{0,1:T(8,128)S(1)} fusion(bf16[2048,2048]{1,0:T(8,128)(2,1)} %bitcast.10, bf16[2048,176]{0,1:T(8,128)(2,1)S(1)} %copy-done.10, bf16[2048,176]{0,1:T(8,128)(2,1)S(1)} %copy-done.11), kind=kOutput, calls=%fused_computation.57 | convolution fusion | flops 2955673600 | bytes 12713984 | tf_op jit(solution)/shard_map/dot_general | solution.py:169
  295.5 3.3 collective-permute-start.13
  298.7 3.7 %collective-permute-done.1 = bf16[2,128,512]{2,1,0:T(8,128)(2,1)S(1)} collective-permute-done((bf16[2,128,512]{2,1,0:T(8,128)(2,1)S(1)}, bf16[2,128,512]{2,1,0:T(8,128)(2,1)S(1)}, u32[]{:S(2)}, u32[]{:S(2)}) %collective-permute-start.1) | collective-permute-done | bytes 262176 | tf_op jit(solution)/shard_map/ppermute | solution.py:80
  302.7 3.3 collective-permute-start.5
  313.9 3.3 collective-permute-start.6
  320.2 3.3 collective-permute-done.3
  327.4 3.4 scatter_fusion
  (145 shorter events, 68.9 us)
Async XLA Ops:
  7.2 58.1 %all-gather.3.cloned.1.call-start = ((), (), s32[]{:S(2)}) async-start(), calls=%async_computation.2 | async-start | bytes 8912896 | tf_op jit(solution)/shard_map/all_gather | solution.py:126
  10.5 115.9 %all-gather.5.cloned.1.call-start = ((), (), s32[]{:S(2)}) async-start(), calls=%async_computation.3 | async-start | bytes 8912896 | tf_op jit(solution)/shard_map/all_gather | solution.py:127
  82.5 43.9 %copy-start = (bf16[128,2048]{1,0:T(8,128)(2,1)S(1)}, bf16[128,2048]{1,0:T(8,128)(2,1)}, u32[]{:S(2)}) copy-start(bf16[128,2048]{1,0:T(8,128)(2,1)} %param.21) | copy-start | bytes 1572868
  135.6 100.2 %all-to-all-start.1 = ((bf16[16,128,2048]{2,1,0:T(8,128)(2,1)}), bf16[16,128,2048]{2,1,0:T(8,128)(2,1)}, u32[]{:S(2)}, u32[]{:S(2)}) async-start(bf16[16,128,2048]{2,1,0:T(8,128)(2,1)} %stack.8), calls=%async_computation.1 | async-start | bytes 16777216 | tf_op jit(solution)/shard_map/all_to_all | solution.py:147
  235.9 14.2 %slice-start = ((s8[5767168]{0:T(1024)(128)(4,1)}), s8[4194304]{0:T(1024)(128)(4,1)S(1)}, s32[]{:S(2)}) async-start(s8[5767168]{0:T(1024)(128)(4,1)} %bitcast.200), calls=%async_computation.4 | async-start | bytes 8388608
  240.7 16.5 %slice-start.2 = ((s8[5767168]{0:T(1024)(128)(4,1)}), s8[4194304]{0:T(1024)(128)(4,1)S(1)}, s32[]{:S(2)}) async-start(s8[5767168]{0:T(1024)(128)(4,1)} %bitcast.202), calls=%async_computation.6 | async-start | bytes 8388608
  275.6 5.8 %collective-permute-start.8 = (bf16[4,2,128,1024]{3,2,1,0:T(8,128)(2,1)}, bf16[4,2,128,1024]{3,2,1,0:T(8,128)(2,1)}, u32[]{:S(2)}, u32[]{:S(2)}) collective-permute-start(bf16[4,2,128,1024]{3,2,1,0:T(8,128)(2,1)} %dynamic-slice_bitcast_fusion), channel_id=1, source_target_pairs={{0,1},{1,0},{2,3},{3,2},{4,5},{5,4},{6,7},{7,6},{8,9},{9,8},{10,11... | collective-permute-start | bytes 6291464 | tf_op jit(solution)/shard_map/ppermute | solution.py:68
  280.8 7.9 %collective-permute-start = (bf16[4,2,128,1024]{3,2,1,0:T(8,128)(2,1)S(1)}, bf16[4,2,128,1024]{3,2,1,0:T(8,128)(2,1)}, u32[]{:S(2)}, u32[]{:S(2)}) collective-permute-start(bf16[4,2,128,1024]{3,2,1,0:T(8,128)(2,1)S(1)} %dynamic-slice_bitcast_fusion.1), channel_id=1, source_target_pairs={{0,1},{1,0},{2,3},{3,2},{4,5},{5,4},{6,7},{7,6},{8,9},{9,8},{10,11... | collective-permute-start | bytes 6291464 | tf_op jit(solution)/shard_map/ppermute | solution.py:68
  285.3 10.0 %collective-permute-start.9 = (bf16[2,128,512]{2,1,0:T(8,128)(2,1)S(1)}, bf16[2,128,512]{2,1,0:T(8,128)(2,1)S(1)}, u32[]{:S(2)}, u32[]{:S(2)}) collective-permute-start(bf16[2,128,512]{2,1,0:T(8,128)(2,1)S(1)} %fusion.83), channel_id=1, source_target_pairs={{0,4},{1,5},{2,6},{3,7},{4,8},{5,9},{6,10},{7,11},{8,12},{9,13},{1... | collective-permute-start | bytes 786440 | tf_op jit(solution)/shard_map/ppermute | solution.py:80
  285.6 9.7 %collective-permute-start.12 = (bf16[2,128,512]{2,1,0:T(8,128)(2,1)S(1)}, bf16[2,128,512]{2,1,0:T(8,128)(2,1)S(1)}, u32[]{:S(2)}, u32[]{:S(2)}) collective-permute-start(bf16[2,128,512]{2,1,0:T(8,128)(2,1)S(1)} %fusion.84), channel_id=1, source_target_pairs={{0,12},{1,13},{2,14},{3,15},{4,0},{5,1},{6,2},{7,3},{8,4},{9,5},{1... | collective-permute-start | bytes 786440 | tf_op jit(solution)/shard_map/ppermute | solution.py:81
  291.9 10.5 %collective-permute-start.1 = (bf16[2,128,512]{2,1,0:T(8,128)(2,1)S(1)}, bf16[2,128,512]{2,1,0:T(8,128)(2,1)S(1)}, u32[]{:S(2)}, u32[]{:S(2)}) collective-permute-start(bf16[2,128,512]{2,1,0:T(8,128)(2,1)S(1)} %fusion.81), channel_id=1, source_target_pairs={{0,4},{1,5},{2,6},{3,7},{4,8},{5,9},{6,10},{7,11},{8,12},{9,13},{1... | collective-permute-start | bytes 786440 | tf_op jit(solution)/shard_map/ppermute | solution.py:80
  292.0 10.6 %collective-permute-start.4 = (bf16[2,128,512]{2,1,0:T(8,128)(2,1)S(1)}, bf16[2,128,512]{2,1,0:T(8,128)(2,1)S(1)}, u32[]{:S(2)}, u32[]{:S(2)}) collective-permute-start(bf16[2,128,512]{2,1,0:T(8,128)(2,1)S(1)} %fusion.82), channel_id=1, source_target_pairs={{0,12},{1,13},{2,14},{3,15},{4,0},{5,1},{6,2},{7,3},{8,4},{9,5},{1... | collective-permute-start | bytes 786440 | tf_op jit(solution)/shard_map/ppermute | solution.py:81
  295.3 12.7 %collective-permute-start.10 = (bf16[2,128,512]{2,1,0:T(8,128)(2,1)S(1)}, bf16[2,128,512]{2,1,0:T(8,128)(2,1)S(1)}, u32[]{:S(2)}, u32[]{:S(2)}) collective-permute-start(bf16[2,128,512]{2,1,0:T(8,128)(2,1)S(1)} %fusion.70), channel_id=1, source_target_pairs={{0,4},{1,5},{2,6},{3,7},{4,8},{5,9},{6,10},{7,11},{8,12},{9,13},{1... | collective-permute-start | bytes 786440 | tf_op jit(solution)/shard_map/ppermute | solution.py:80
  295.5 13.0 %collective-permute-start.13 = (bf16[2,128,512]{2,1,0:T(8,128)(2,1)S(1)}, bf16[2,128,512]{2,1,0:T(8,128)(2,1)S(1)}, u32[]{:S(2)}, u32[]{:S(2)}) collective-permute-start(bf16[2,128,512]{2,1,0:T(8,128)(2,1)S(1)} %fusion.68), channel_id=1, source_target_pairs={{0,12},{1,13},{2,14},{3,15},{4,0},{5,1},{6,2},{7,3},{8,4},{9,5},{1... | collective-permute-start | bytes 786440 | tf_op jit(solution)/shard_map/ppermute | solution.py:81
  302.5 11.2 %collective-permute-start.2 = (bf16[2,128,512]{2,1,0:T(8,128)(2,1)S(1)}, bf16[2,128,512]{2,1,0:T(8,128)(2,1)S(1)}, u32[]{:S(2)}, u32[]{:S(2)}) collective-permute-start(bf16[2,128,512]{2,1,0:T(8,128)(2,1)S(1)} %fusion.74), channel_id=1, source_target_pairs={{0,4},{1,5},{2,6},{3,7},{4,8},{5,9},{6,10},{7,11},{8,12},{9,13},{1... | collective-permute-start | bytes 786440 | tf_op jit(solution)/shard_map/ppermute | solution.py:80
  302.7 11.1 %collective-permute-start.5 = (bf16[2,128,512]{2,1,0:T(8,128)(2,1)S(1)}, bf16[2,128,512]{2,1,0:T(8,128)(2,1)S(1)}, u32[]{:S(2)}, u32[]{:S(2)}) collective-permute-start(bf16[2,128,512]{2,1,0:T(8,128)(2,1)S(1)} %fusion.72), channel_id=1, source_target_pairs={{0,12},{1,13},{2,14},{3,15},{4,0},{5,1},{6,2},{7,3},{8,4},{9,5},{1... | collective-permute-start | bytes 786440 | tf_op jit(solution)/shard_map/ppermute | solution.py:81
  308.1 11.2 %collective-permute-start.11 = (bf16[2,128,512]{2,1,0:T(8,128)(2,1)S(1)}, bf16[2,128,512]{2,1,0:T(8,128)(2,1)S(1)}, u32[]{:S(2)}, u32[]{:S(2)}) collective-permute-start(bf16[2,128,512]{2,1,0:T(8,128)(2,1)S(1)} %fusion.69), channel_id=1, source_target_pairs={{0,4},{1,5},{2,6},{3,7},{4,8},{5,9},{6,10},{7,11},{8,12},{9,13},{1... | collective-permute-start | bytes 786440 | tf_op jit(solution)/shard_map/ppermute | solution.py:80
  308.5 10.8 %collective-permute-start.14 = (bf16[2,128,512]{2,1,0:T(8,128)(2,1)S(1)}, bf16[2,128,512]{2,1,0:T(8,128)(2,1)S(1)}, u32[]{:S(2)}, u32[]{:S(2)}) collective-permute-start(bf16[2,128,512]{2,1,0:T(8,128)(2,1)S(1)} %fusion.67), channel_id=1, source_target_pairs={{0,12},{1,13},{2,14},{3,15},{4,0},{5,1},{6,2},{7,3},{8,4},{9,5},{1... | collective-permute-start | bytes 786440 | tf_op jit(solution)/shard_map/ppermute | solution.py:81
  313.7 9.8 %collective-permute-start.3 = (bf16[2,128,512]{2,1,0:T(8,128)(2,1)S(1)}, bf16[2,128,512]{2,1,0:T(8,128)(2,1)S(1)}, u32[]{:S(2)}, u32[]{:S(2)}) collective-permute-start(bf16[2,128,512]{2,1,0:T(8,128)(2,1)S(1)} %fusion.73), channel_id=1, source_target_pairs={{0,4},{1,5},{2,6},{3,7},{4,8},{5,9},{6,10},{7,11},{8,12},{9,13},{1... | collective-permute-start | bytes 786440 | tf_op jit(solution)/shard_map/ppermute | solution.py:80
  313.9 11.2 %copy-start.4 = (bf16[2048,128]{1,0:T(8,128)(2,1)S(1)}, bf16[2048,128]{1,0:T(8,128)(2,1)}, u32[]{:S(2)}) copy-start(bf16[2048,128]{1,0:T(8,128)(2,1)} %get-tuple-element.114) | copy-start | bytes 1572868
  313.9 11.2 %copy-start.5 = (bf16[2048,128]{1,0:T(8,128)(2,1)S(1)}, bf16[2048,128]{1,0:T(8,128)(2,1)}, u32[]{:S(2)}) copy-start(bf16[2048,128]{1,0:T(8,128)(2,1)} %get-tuple-element.117) | copy-start | bytes 1572868
  313.9 9.7 %collective-permute-start.6 = (bf16[2,128,512]{2,1,0:T(8,128)(2,1)S(1)}, bf16[2,128,512]{2,1,0:T(8,128)(2,1)S(1)}, u32[]{:S(2)}, u32[]{:S(2)}) collective-permute-start(bf16[2,128,512]{2,1,0:T(8,128)(2,1)S(1)} %fusion.71), channel_id=1, source_target_pairs={{0,12},{1,13},{2,14},{3,15},{4,0},{5,1},{6,2},{7,3},{8,4},{9,5},{1... | collective-permute-start | bytes 786440 | tf_op jit(solution)/shard_map/ppermute | solution.py:81
  319.5 11.3 %collective-permute-start.15 = (bf16[128,1024]{1,0:T(8,128)(2,1)S(1)}, bf16[128,1024]{1,0:T(8,128)(2,1)}, u32[]{:S(2)}, u32[]{:S(2)}) collective-permute-start(bf16[128,1024]{1,0:T(8,128)(2,1)S(1)} %fusion.86), channel_id=1, source_target_pairs={{0,2},{1,3},{2,0},{3,1},{4,6},{5,7},{6,4},{7,5},{8,10},{9,11},{10,... | collective-permute-start | bytes 786440 | tf_op jit(solution)/shard_map/ppermute | solution.py:96
  324.4 7.3 %collective-permute-start.7 = (bf16[128,1024]{1,0:T(8,128)(2,1)}, bf16[128,1024]{1,0:T(8,128)(2,1)}, u32[]{:S(2)}, u32[]{:S(2)}) collective-permute-start(bf16[128,1024]{1,0:T(8,128)(2,1)} %fusion.85), channel_id=1, source_target_pairs={{0,2},{1,3},{2,0},{3,1},{4,6},{5,7},{6,4},{7,5},{8,10},{9,11},{10,... | collective-permute-start | bytes 786440 | tf_op jit(solution)/shard_map/ppermute | solution.py:96
  (13 other events, 55.2 us)
Sparse Core Ops, SparseCore 0:
  10.6 54.5 all-gather.2
  66.9 58.6 all-gather.4
